TPU v7x, 32 devices: a whole 2x2x4 slice. The times are simulated.
32 devices in a mesh: rep: 8 (over z, x), tile: 4 (over y, core).
Axes of the slice: x: 2, y: 2, z: 4, core: 2. Of those that a mesh axis runs over, the one named last changes fastest.
Arguments:
- features: bfloat16 [16, 48, 72, 1536], P('rep', 'tile'), may hold values from -6 to 6
- conv_out: bfloat16 [16, 48, 72, 256], P('rep', 'tile'), may hold values from -6 to 6
- conv_weight: bfloat16 [9, 1536, 256], replicated, may hold values from -0.0546875 to 0.0546875
- norm_gain_vector: float32 [256], replicated, may hold values from 0.5 to 1.5
- norm_shift_vector: float32 [256], replicated, may hold values from -3 to 3
- class_map: float32 [3, 256], replicated, may hold values from -3 to 3
- labels: int32 [16, 48, 72], P('rep', 'tile'), may hold values from 0 to 2
- class_weight: int32 [3], replicated, may hold values from 1 to 39
Outputs:
- grad_features: bfloat16 [16, 48, 72, 1536], P('rep', 'tile')
- grad_weight: float32 [1536, 9, 256], P(('rep', 'tile'))
- grad_gain: float32 [256], replicated
- grad_shift: float32 [256], replicated
- grad_class: float32 [3, 256], replicated
- loss: float32 [], replicated
All inputs are finite; a program needn't handle non-finite values.
Results may differ from a plain program's by a relative error of at most 0.0049.
Values may be sent and summed in bfloat16 or wider, within the bound.
No kernel may reach another device: no remote copies, remote signals or barrier semaphores. Data moves between devices by JAX's collectives and lax.ppermute only.
A program may use at most 256 MiB of HBM per device.

v0:
```python
import jax
import jax.numpy as jnp
from jax import lax
from jax.sharding import PartitionSpec as P

IMG_DEV = 2
H = 48
W = 72
RATE = 12


def padded(x, sides, width):
    for axis, dim in sides:
        size, length = (lax.axis_size(axis), x.shape[dim])
        up = [(i, (i + 1) % size) for i in range(size - 1)]
        down = [(j, i) for i, j in up]
        last = lax.slice_in_dim(x, length - width, length, axis=dim)
        first = lax.slice_in_dim(x, 0, width, axis=dim)
        before = lax.ppermute(last, axis, up)
        after = lax.ppermute(first, axis, down)
        x = jnp.concatenate([before, x, after], axis=dim)
    return x


def body(
    features,
    conv_out,
    conv_weight,
    norm_gain_vector,
    norm_shift_vector,
    class_map,
    labels,
    class_weight,
):
    highest = lax.Precision.HIGHEST
    images, tile_rows, columns, in_chans = features.shape
    out_chans = conv_out.shape[3]
    local_pix = images * tile_rows * columns
    per_replica_part = IMG_DEV * H * W
    all_pix = lax.axis_size("rep") * per_replica_part
    yvals = conv_out.astype(jnp.float32).reshape(local_pix, out_chans)
    column_sum = lax.psum(jnp.sum(yvals, 0), "tile")
    centre_offset = yvals - column_sum / per_replica_part
    variance = lax.psum(jnp.sum(centre_offset * centre_offset, 0), "tile") / per_replica_part
    inverse_deviation = lax.rsqrt(variance + 1e-05)
    normalized_input = centre_offset * inverse_deviation
    preactivation_values = norm_gain_vector * normalized_input + norm_shift_vector
    zvals = jnp.maximum(preactivation_values, 0.0)
    logits = jnp.dot(zvals, class_map.T, precision=highest)
    onehot = (
        labels.reshape(local_pix, 1) == jnp.arange(class_map.shape[0], dtype=jnp.int32)
    ).astype(jnp.float32)
    weights_pix = jnp.sum(onehot * class_weight.astype(jnp.float32), -1)
    top_val = jnp.max(logits, -1, keepdims=True)
    log_total = top_val[:, 0] + jnp.log(jnp.sum(jnp.exp(logits - top_val), -1))
    cross = log_total - jnp.sum(onehot * logits, -1)
    weight_total, loss_total = lax.psum(
        (jnp.sum(weights_pix), jnp.sum(weights_pix * cross)), ("rep", "tile")
    )
    mean_weight = weight_total / all_pix
    loss = loss_total / mean_weight / all_pix
    probs = jnp.exp(logits - log_total[:, None])
    grad_logit = (weights_pix / mean_weight)[:, None] * (probs - onehot)
    class_local_slice = jnp.dot(grad_logit.T, zvals, precision=highest)
    grad_z = jnp.dot(grad_logit, class_map, precision=highest)
    preactivation_gradient = jnp.where(preactivation_values > 0, grad_z, 0.0)
    first_gradient_sum, second_gradient_sum, class_tile = lax.psum(
        (
            jnp.sum(preactivation_gradient, 0),
            jnp.sum(preactivation_gradient * normalized_input, 0),
            class_local_slice,
        ),
        "tile",
    )
    grad_shift, grad_gain, grad_class = lax.psum(
        (first_gradient_sum, second_gradient_sum, class_tile), "rep"
    )
    normalized_output_gradient = (
        norm_gain_vector
        * inverse_deviation
        * (
            preactivation_gradient
            - first_gradient_sum / per_replica_part
            - normalized_input * second_gradient_sum / per_replica_part
        )
    ).astype(jnp.bfloat16)
    normalized_output_gradient = normalized_output_gradient.reshape(
        images, tile_rows, columns, out_chans
    )
    extended = padded(normalized_output_gradient, (("tile", 1),), RATE)
    extended = jnp.pad(extended, ((0, 0), (0, 0), (RATE, RATE), (0, 0)))
    shifted_list = []
    for tap_index in range(9):
        row_off = RATE - (tap_index // 3 - 1) * RATE
        col_off = RATE - (tap_index % 3 - 1) * RATE
        piece = extended[:, row_off : row_off + tile_rows, col_off : col_off + columns, :]
        shifted_list.append(piece.reshape(local_pix, out_chans))
    accum_grad = jnp.zeros((local_pix, in_chans), jnp.float32)
    for tap_index in range(9):
        accum_grad = accum_grad + lax.dot_general(
            shifted_list[tap_index],
            conv_weight[tap_index],
            (((1,), (1,)), ((), ())),
            preferred_element_type=jnp.float32,
        )
    grad_features = accum_grad.astype(jnp.bfloat16).reshape(images, tile_rows, columns, in_chans)
    flat_x = features.reshape(local_pix, in_chans)
    parts_list = [
        lax.dot_general(
            flat_x, shifted, (((0,), (0,)), ((), ())), preferred_element_type=jnp.float32
        )
        for shifted in shifted_list
    ]
    grad_weight = lax.psum_scatter(
        jnp.stack(parts_list, 1), ("rep", "tile"), scatter_dimension=0, tiled=True
    )
    return (grad_features, grad_weight, grad_gain, grad_shift, grad_class, loss)


def solution(mesh):
    in_specs = (
        P("rep", "tile", None, None),
        P("rep", "tile", None, None),
        P(),
        P(),
        P(),
        P(),
        P("rep", "tile", None),
        P(),
    )
    out_specs = (P("rep", "tile", None, None), P(("rep", "tile"), None, None), P(), P(), P(), P())
    return jax.shard_map(body, mesh=mesh, in_specs=in_specs, out_specs=out_specs, check_vma=False)
```

profile of v0, /device:TPU:0, one launch (start us, length us, event | category | flops | bytes accessed | tf_op | source)
XLA Modules:
  0.0 405.0 jit_solution(10787423601491690530)
XLA Ops:
  7.2 0.0 copy-start
  7.2 0.0 reduce-scatter.2.cloned.1.call-start
  7.3 1.4 convert_reduce_fusion
  8.7 8.4 %psum.70 = f32[256]{0:T(256)S(1)} all-reduce(f32[256]{0:T(256)S(1)} %convert_reduce_fusion), channel_id=1, replica_groups=mesh['rep'=8,'tile'=4] {'tile'}, use_global_device_ids=true, to_apply=%region_1.0 | all-reduce | flops 256 | bytes 2048 | tf_op jit(solution)/shard_map/psum | solution.py:42
  17.0 1.5 multiply_reduce_fusion.1
  18.5 5.8 %psum.71 = f32[256]{0:T(256)S(1)} all-reduce(f32[256]{0:T(256)S(1)} %multiply_reduce_fusion.1), channel_id=1, replica_groups=mesh['rep'=8,'tile'=4] {'tile'}, use_global_device_ids=true, to_apply=%region_3.0 | all-reduce | flops 256 | bytes 2048 | tf_op jit(solution)/shard_map/psum | solution.py:44
  24.2 0.7 fusion.54
  24.9 1.3 fusion.15
  26.3 0.7 copy.17
  27.0 0.1 eq.15
  27.1 0.7 convert_element_type.18
  27.7 2.5 fusion.63
  30.2 0.7 select_reduce_fusion.2
  30.9 0.6 multiply_reduce_fusion.2
  31.5 39.9 %all-reduce.1 = (f32[]{:T(128)}, f32[]{:T(128)}) all-reduce(f32[]{:T(128)} %get-tuple-element.31, f32[]{:T(128)} %get-tuple-element.40), channel_id=1, replica_groups=mesh['rep'=8,'tile'=4] {'rep','tile'}, use_global_device_ids=true, to_apply=%region_6.0 | all-reduce | flops 2 | bytes 16 | tf_op jit(solution)/shard_map/psum | solution.py:57
  72.1 1.0 fusion.16
  73.1 4.6 %fusion.61 = (f32[256]{0:T(256)S(1)}, f32[256]{0:T(256)S(1)}, f32[1728,256]{1,0:T(8,128)}) fusion(f32[256]{0:T(256)S(1)} %get-tuple-element.49, f32[256]{0:T(256)S(1)} %broadcast_multiply_fusion.1, bf16[2,12,72,256]{3,2,1,0:T(8,128)(2,1)} %param.9, f32[3,256]{1,0:T(4,128)S(1)} %copy-done, f32[1728,3]{0,1:T(4,128)S(1)} %get-tuple-element.51, ...), kind=kOutput, calls=%fused_computation.92 | convolution fusion | flops 20374336 | bytes 4474368 | tf_op jit(solution)/shard_map/dot_general | solution.py:65
  77.6 6.9 %all-reduce.3 = (f32[256]{0:T(256)S(1)}, f32[256]{0:T(256)S(1)}, f32[3,256]{1,0:T(4,128)S(1)}) all-reduce(f32[256]{0:T(256)S(1)} %get-tuple-element.25, f32[256]{0:T(256)S(1)} %get-tuple-element.24, f32[3,256]{1,0:T(4,128)S(1)} %fusion.16), channel_id=1, replica_groups=mesh['rep'=8,'tile'=4] {'tile'}, use_global_device_ids=true, to_apply=%region_12.13 | all-reduce | flops 1280 | bytes 10240 | tf_op jit(solution)/shard_map/psum | solution.py:67
  84.5 2.3 multiply_convert_fusion
  86.9 1.5 collective-permute-start
  88.4 1.5 collective-permute-start.1
  89.9 0.5 collective-permute-done
  90.4 3.8 collective-permute-done.1
  94.2 1.8 fusion.5
  96.1 2.8 fusion.14
  98.9 2.8 fusion.13
  101.7 2.8 fusion.12
  104.4 2.8 fusion.11
  107.2 2.8 fusion.10
  110.0 2.8 fusion.9
  112.7 2.7 fusion.8
  115.5 2.8 fusion.7
  118.3 2.8 fusion.6
  121.0 19.0 %copy.18 = f32[1536,9,256]{2,1,0:T(8,128)} copy(f32[1536,9,256]{0,2,1:T(8,128)} %fusion.6) | data formatting | bytes 28311552 | tf_op jit(solution)/shard_map/stack | solution.py:115
  140.0 0.0 reduce-scatter.2.cloned.1.call-update
  140.7 21.3 %all-reduce.2 = (f32[256]{0:T(256)}, f32[256]{0:T(256)}, f32[3,256]{1,0:T(4,128)}) all-reduce(f32[256]{0:T(256)S(1)} %get-tuple-element.37, f32[256]{0:T(256)S(1)} %get-tuple-element.38, f32[3,256]{1,0:T(4,128)S(1)} %get-tuple-element.39), channel_id=1, replica_groups=mesh['rep'=8,'tile'=4] {'rep'}, use_global_device_ids=true, to_apply=%region_14.15 | all-reduce | flops 1280 | bytes 10240 | tf_op jit(solution)/shard_map/psum | solution.py:75
  162.0 7.7 %fusion.33 = f32[1728,1536]{1,0:T(8,128)} fusion(bf16[1728,256]{1,0:T(8,128)(2,1)S(1)} %multiply_convert_fusion, bf16[9,1536,256]{2,1,0:T(8,128)(2,1)} %param.10), kind=kOutput, calls=%fused_computation.52 | convolution fusion | flops 1358954496 | bytes 12288000 | tf_op jit(solution)/shard_map/dot_general | solution.py:100
  169.7 0.6 fusion.62
  170.3 8.2 %fusion.26 = f32[1728,1536]{1,0:T(8,128)} fusion(bf16[1728,256]{1,0:T(8,128)(2,1)S(1)} %bitcast.174, bf16[9,1536,256]{2,1,0:T(8,128)(2,1)} %param.10), kind=kOutput, calls=%fused_computation.45 | convolution fusion | flops 1358954496 | bytes 12288000 | tf_op jit(solution)/shard_map/dot_general | solution.py:100
  178.5 6.4 %fusion.29 = f32[1728,1536]{1,0:T(8,128)} fusion(bf16[1728,256]{1,0:T(8,128)(2,1)S(1)} %bitcast.173, bf16[9,1536,256]{2,1,0:T(8,128)(2,1)S(1)} %bitcast.167), kind=kOutput, calls=%fused_computation.48 | convolution fusion | flops 1358954496 | bytes 12288000 | tf_op jit(solution)/shard_map/dot_general | solution.py:100
  184.9 6.3 %fusion.31 = f32[1728,1536]{1,0:T(8,128)} fusion(bf16[1728,256]{1,0:T(8,128)(2,1)S(1)} %bitcast.172, bf16[9,1536,256]{2,1,0:T(8,128)(2,1)S(1)} %bitcast.167), kind=kOutput, calls=%fused_computation.50 | convolution fusion | flops 1358954496 | bytes 12288000 | tf_op jit(solution)/shard_map/dot_general | solution.py:100
  191.2 6.3 %fusion.35 = f32[1728,1536]{1,0:T(8,128)} fusion(bf16[1728,256]{1,0:T(8,128)(2,1)S(1)} %bitcast.171, bf16[9,1536,256]{2,1,0:T(8,128)(2,1)S(1)} %bitcast.167), kind=kOutput, calls=%fused_computation.54 | convolution fusion | flops 1358954496 | bytes 12288000 | tf_op jit(solution)/shard_map/dot_general | solution.py:100
  197.6 5.7 %fusion.37 = f32[1728,1536]{1,0:T(8,128)} fusion(bf16[1728,256]{1,0:T(8,128)(2,1)S(1)} %bitcast.170, bf16[9,1536,256]{2,1,0:T(8,128)(2,1)S(1)} %bitcast.167), kind=kOutput, calls=%fused_computation.56 | convolution fusion | flops 1358954496 | bytes 12288000 | tf_op jit(solution)/shard_map/dot_general | solution.py:100
  203.3 5.6 %fusion.41 = f32[1728,1536]{1,0:T(8,128)} fusion(bf16[1728,256]{1,0:T(8,128)(2,1)S(1)} %bitcast.169, bf16[9,1536,256]{2,1,0:T(8,128)(2,1)S(1)} %bitcast.167), kind=kOutput, calls=%fused_computation.60 | convolution fusion | flops 1358954496 | bytes 12288000 | tf_op jit(solution)/shard_map/dot_general | solution.py:100
  209.0 6.2 %fusion.39 = f32[1728,1536]{1,0:T(8,128)} fusion(bf16[1728,256]{1,0:T(8,128)(2,1)S(1)} %bitcast.164, bf16[9,1536,256]{2,1,0:T(8,128)(2,1)S(1)} %bitcast.167), kind=kOutput, calls=%fused_computation.58 | convolution fusion | flops 1358954496 | bytes 12288000 | tf_op jit(solution)/shard_map/dot_general | solution.py:100
  215.1 30.1 %add_convert_fusion = bf16[1728,1536]{1,0:T(8,128)(2,1)} fusion(f32[1728,1536]{1,0:T(8,128)} %fusion.26, f32[1728,1536]{1,0:T(8,128)} %fusion.29, f32[1728,1536]{1,0:T(8,128)} %fusion.31, f32[1728,1536]{1,0:T(8,128)} %fusion.33, f32[1728,1536]{1,0:T(8,128)} %fusion.35, f32[1728,1536]{1,0:T(8,128)} %fusion.37, f32[1728,1536]{1,0:T(8,128)} %fusion.41, ...), kind=kOutput, calls=%fused_computation.2 | convolution fusion | flops 1382842368 | bytes 91914240 | tf_op jit(solution)/shard_map/dot_general | solution.py:100
  245.2 149.6 %reduce-scatter.2.cloned.1.call-done = f32[48,9,256]{2,1,0:T(8,128)} async-done(((f32[1536,9,256]{2,1,0:T(8,128)}), f32[48,9,256]{2,1,0:T(8,128)}) %reduce-scatter.2.cloned.1.call-update) | async-done | bytes 442384 | tf_op jit(solution)/shard_map/reduce_scatter | solution.py:114
  394.8 2.2 copy.19
  (28 shorter events, 0.1 us)
Async XLA Ops:
  7.2 20.6 %copy-start = (f32[3,256]{1,0:T(4,128)S(1)}, f32[3,256]{1,0:T(4,128)}, u32[]{:S(2)}) copy-start(f32[3,256]{1,0:T(4,128)} %param.13) | copy-start | bytes 9220
  7.2 64.9 %copy-start.6 = (f32[256]{0:T(256)S(1)}, f32[256]{0:T(256)}, u32[]{:S(2)}) copy-start(f32[256]{0:T(256)} %param.11) | copy-start | bytes 3076
  7.2 64.9 %copy-start.7 = (f32[256]{0:T(256)S(1)}, f32[256]{0:T(256)}, u32[]{:S(2)}) copy-start(f32[256]{0:T(256)} %param.12) | copy-start | bytes 3076
  7.2 387.6 %reduce-scatter.2.cloned.1.call-start = ((), (), s32[]{:S(2)}) async-start(), calls=%async_computation.1 | async-start | bytes 25952256 | tf_op jit(solution)/shard_map/reduce_scatter | solution.py:114
  73.1 23.0 %slice-start = ((s8[5308416]{0:T(1024)(128)(4,1)}), s8[1114112]{0:T(1024)(128)(4,1)S(1)}, s32[]{:S(2)}) async-start(s8[5308416]{0:T(1024)(128)(4,1)} %bitcast.158), calls=%async_computation.2 | async-start | bytes 2228224
  84.5 11.5 %slice-start.1 = ((s8[5308416]{0:T(1024)(128)(4,1)}), s8[4194304]{0:T(1024)(128)(4,1)S(1)}, s32[]{:S(2)}) async-start(s8[5308416]{0:T(1024)(128)(4,1)} %bitcast.158), calls=%async_computation.3 | async-start | bytes 8388608
  86.9 3.5 collective-permute-start
  88.4 5.8 %collective-permute-start.1 = (bf16[2,12,72,256]{3,2,1,0:T(8,128)(2,1)S(1)}, bf16[2,12,72,256]{3,2,1,0:T(8,128)(2,1)S(1)}, u32[]{:S(2)}, u32[]{:S(2)}) collective-permute-start(bf16[2,12,72,256]{3,2,1,0:T(8,128)(2,1)S(1)} %bitcast.161), channel_id=1, source_target_pairs={{1,0},{2,1},{3,2},{5,4},{6,5},{7,6},{9,8},{10,9},{11,10},{13,12},{... | collective-permute-start | bytes 2654216 | tf_op jit(solution)/shard_map/ppermute | solution.py:20
  90.4 25.1 %copy-start.4 = (bf16[2,12,72,256]{3,2,1,0:T(8,128)(2,1)}, bf16[2,12,72,256]{3,2,1,0:T(8,128)(2,1)S(1)}, u32[]{:S(2)}) copy-start(bf16[2,12,72,256]{3,2,1,0:T(8,128)(2,1)S(1)} %collective-permute-done) | copy-start | bytes 2654212
  96.0 22.2 %copy-start.2 = (bf16[2,36,96,256]{3,2,1,0:T(8,128)(2,1)}, bf16[2,36,96,256]{3,2,1,0:T(8,128)(2,1)S(1)}, u32[]{:S(2)}) copy-start(bf16[2,36,96,256]{3,2,1,0:T(8,128)(2,1)S(1)} %fusion.5) | copy-start | bytes 10616836
  162.0 7.7 %copy-start.3 = (bf16[2,36,96,256]{3,2,1,0:T(8,128)(2,1)S(1)}, bf16[2,36,96,256]{3,2,1,0:T(8,128)(2,1)}, u32[]{:S(2)}) copy-start(bf16[2,36,96,256]{3,2,1,0:T(8,128)(2,1)} %copy-done.2) | copy-start | bytes 10616836
  169.7 8.8 %slice-start.2 = ((s8[7077888]{0:T(1024)(128)(4,1)}), s8[2883584]{0:T(1024)(128)(4,1)S(1)}, s32[]{:S(2)}) async-start(s8[7077888]{0:T(1024)(128)(4,1)} %bitcast.166), calls=%async_computation.4 | async-start | bytes 5767168
  170.3 8.2 %slice-start.3 = ((s8[7077888]{0:T(1024)(128)(4,1)}), s8[4194304]{0:T(1024)(128)(4,1)S(1)}, s32[]{:S(2)}) async-start(s8[7077888]{0:T(1024)(128)(4,1)} %bitcast.166), calls=%async_computation.5 | async-start | bytes 8388608
  208.9 6.2 %copy-start.5 = (bf16[2,12,72,256]{3,2,1,0:T(8,128)(2,1)S(1)}, bf16[2,12,72,256]{3,2,1,0:T(8,128)(2,1)}, u32[]{:S(2)}) copy-start(bf16[2,12,72,256]{3,2,1,0:T(8,128)(2,1)} %copy-done.4) | copy-start | bytes 2654212
  215.1 181.9 %copy-start.1 = (f32[3,256]{1,0:T(4,128)S(1)}, f32[3,256]{1,0:T(4,128)}, u32[]{:S(2)}) copy-start(f32[3,256]{1,0:T(4,128)} %param.13) | copy-start | bytes 9220
Sparse Core Ops, SparseCore 0:
  140.1 254.6 reduce-scatter.1
where the time goes:
time: 406 us; the launch traced here: 405 us
  waiting for transfers between devices  154 us (38%)
  matrix products  116 us (29%)
  blocking collectives  82.2 us (20%)
  local copies, waits for them, and re-layouts  22.6 us (6%)
  between operations  16.6 us (4%)
  other arithmetic  11.1 us (3%)
    reduce_scatter x1, waiting for transfers between devices, body(): lax.psum_scatter(jnp.stack(parts_list, 1), ('rep', 'tile'), scatter_dimen...  150 us
    dot_general x9, matrix products, body(): lax.dot_general(shifted_list[tap_index], conv_weight[tap_index], (((1,),...  82.6 us
    psum x1, blocking collectives, body(): lax.psum((jnp.sum(weights_pix), jnp.sum(weights_pix * cross)), ('rep', 't...  39.9 us
    dot_general x9, matrix products, body(): lax.dot_general(flat_x, shifted, (((0,), (0,)), ((), ())), preferred_elem...  25 us
    psum x1, blocking collectives, body(): lax.psum((first_gradient_sum, second_gradient_sum, class_tile), 'rep')  21.3 us
    another operation x1, local copies, waits for them, and re-layouts, body(): jnp.stack(parts_list, 1)  19 us
    psum x1, blocking collectives, body(): column_sum = lax.psum(jnp.sum(yvals, 0), 'tile')  8.36 us
  transfers between devices with their start and end apart: 3, of which 3 were waited for; matrix products, arithmetic and copies ran while one was open for 21% of the time, Pallas kernels for 0%

commit v1 on v0

--- a/solution.py
+++ b/solution.py
@@ -7,6 +7,11 @@
 H = 48
 W = 72
 RATE = 12
+
+
+def one_after_other(value, leading, second):
+    partial = lax.psum(value, leading)
+    return lax.psum(partial, second)
 
 
 def padded(x, sides, width):
@@ -54,8 +59,8 @@
     top_val = jnp.max(logits, -1, keepdims=True)
     log_total = top_val[:, 0] + jnp.log(jnp.sum(jnp.exp(logits - top_val), -1))
     cross = log_total - jnp.sum(onehot * logits, -1)
-    weight_total, loss_total = lax.psum(
-        (jnp.sum(weights_pix), jnp.sum(weights_pix * cross)), ("rep", "tile")
+    weight_total, loss_total = one_after_other(
+        (jnp.sum(weights_pix), jnp.sum(weights_pix * cross)), "tile", "rep"
     )
     mean_weight = weight_total / all_pix
     loss = loss_total / mean_weight / all_pix

time: 406 us -> 391 us (0.963)
  blocking collectives: 82.2 us -> 67.5 us
    psum x1 -> x2, blocking collectives: 39.9 us -> 28.7 us  [the longest x1 22.4 us: one_after_other(): return lax.psum(partial, second)]
where the time goes in v1:
time: 391 us; the launch traced here: 390 us
  waiting for transfers between devices  153 us (39%)
  matrix products  116 us (30%)
  blocking collectives  67.5 us (17%)
  local copies, waits for them, and re-layouts  22.6 us (6%)
  between operations  16.6 us (4%)
  other arithmetic  11.1 us (3%)
    reduce_scatter x1, waiting for transfers between devices, body(): lax.psum_scatter(jnp.stack(parts_list, 1), ('rep', 'tile'), scatter_dimen...  150 us
    dot_general x9, matrix products, body(): lax.dot_general(shifted_list[tap_index], conv_weight[tap_index], (((1,),...  82.6 us
    dot_general x9, matrix products, body(): lax.dot_general(flat_x, shifted, (((0,), (0,)), ((), ())), preferred_elem...  25 us
    psum x1, blocking collectives, one_after_other(): return lax.psum(partial, second)  22.4 us
    another operation x1, local copies, waits for them, and re-layouts, body(): jnp.stack(parts_list, 1)  19 us
    psum x1, blocking collectives, body(): lax.psum((first_gradient_sum, second_gradient_sum, class_tile), 'rep')  18.3 us
    psum x1, blocking collectives, body(): column_sum = lax.psum(jnp.sum(yvals, 0), 'tile')  8.36 us
  transfers between devices with their start and end apart: 3, of which 3 were waited for; matrix products, arithmetic and copies ran while one was open for 21% of the time, Pallas kernels for 0%

profile of v1, /device:TPU:0, one launch (start us, length us, event | category | flops | bytes accessed | tf_op | source)
XLA Modules:
  0.0 390.1 jit_solution(4579871767185195462)
XLA Ops:
  7.2 0.0 reduce-scatter.2.cloned.1.call-start
  7.3 1.4 convert_reduce_fusion
  8.7 8.4 %psum.84 = f32[256]{0:T(256)S(1)} all-reduce(f32[256]{0:T(256)S(1)} %convert_reduce_fusion), channel_id=1, replica_groups=mesh['rep'=8,'tile'=4] {'tile'}, use_global_device_ids=true, to_apply=%region_1.0 | all-reduce | flops 256 | bytes 2048 | tf_op jit(solution)/shard_map/psum | solution.py:47
  17.0 1.5 multiply_reduce_fusion.1
  18.5 5.8 %psum.85 = f32[256]{0:T(256)S(1)} all-reduce(f32[256]{0:T(256)S(1)} %multiply_reduce_fusion.1), channel_id=1, replica_groups=mesh['rep'=8,'tile'=4] {'tile'}, use_global_device_ids=true, to_apply=%region_3.0 | all-reduce | flops 256 | bytes 2048 | tf_op jit(solution)/shard_map/psum | solution.py:49
  24.2 0.7 fusion.54
  24.9 1.3 fusion.15
  26.3 0.7 copy.17
  27.0 0.1 eq.15
  27.1 0.7 convert_element_type.18
  27.7 2.5 fusion.63
  30.2 0.7 select_reduce_fusion.2
  30.9 6.4 %psum.86 = f32[]{:T(128)} all-reduce(f32[]{:T(128)} %get-tuple-element.31), channel_id=1, replica_groups=mesh['rep'=8,'tile'=4] {'tile'}, use_global_device_ids=true, to_apply=%region_6.0 | all-reduce | flops 1 | bytes 8 | tf_op jit(solution)/shard_map/psum | solution.py:13
  37.2 22.4 %psum.87 = f32[]{:T(128)} all-reduce(f32[]{:T(128)} %psum.86), channel_id=1, replica_groups=mesh['rep'=8,'tile'=4] {'rep'}, use_global_device_ids=true, to_apply=%region_7.0 | all-reduce | flops 1 | bytes 8 | tf_op jit(solution)/shard_map/psum | solution.py:14
  60.2 0.6 multiply_reduce_fusion.2
  60.9 1.0 fusion.16
  61.9 4.6 %fusion.61 = (f32[256]{0:T(256)S(1)}, f32[256]{0:T(256)S(1)}, f32[1728,256]{1,0:T(8,128)}) fusion(f32[256]{0:T(256)S(1)} %get-tuple-element.50, f32[256]{0:T(256)S(1)} %broadcast_multiply_fusion.1, bf16[2,12,72,256]{3,2,1,0:T(8,128)(2,1)} %param.9, f32[3,256]{1,0:T(4,128)S(1)} %copy-done, f32[1728,3]{0,1:T(4,128)S(1)} %get-tuple-element.52, ...), kind=kOutput, calls=%fused_computation.92 | convolution fusion | flops 20374336 | bytes 4474368 | tf_op jit(solution)/shard_map/dot_general | solution.py:70
  66.4 6.4 %all-reduce.2 = (f32[256]{0:T(256)S(1)}, f32[256]{0:T(256)S(1)}, f32[3,256]{1,0:T(4,128)S(1)}, f32[]{:T(128)}) all-reduce(f32[256]{0:T(256)S(1)} %get-tuple-element.25, f32[256]{0:T(256)S(1)} %get-tuple-element.24, f32[3,256]{1,0:T(4,128)S(1)} %fusion.16, f32[]{:T(128)} %get-tuple-element.40), channel_id=1, replica_groups=mesh['rep'=8,'tile'=4] {'tile'}, use_global_device_ids=true, to_apply=%region_13.0 | all-reduce | flops 1281 | bytes 10248 | tf_op jit(solution)/shard_map/psum | solution.py:72
  72.8 2.3 multiply_convert_fusion
  75.2 1.8 collective-permute-start
  77.0 1.5 collective-permute-start.1
  78.4 0.5 collective-permute-done
  78.9 3.3 collective-permute-done.1
  82.2 1.8 fusion.5
  84.1 2.8 fusion.14
  87.0 2.8 fusion.13
  89.7 2.8 fusion.12
  92.5 2.8 fusion.11
  95.3 2.8 fusion.10
  98.1 2.8 fusion.9
  100.8 2.7 fusion.8
  103.6 2.8 fusion.7
  106.3 2.8 fusion.6
  109.1 19.0 %copy.18 = f32[1536,9,256]{2,1,0:T(8,128)} copy(f32[1536,9,256]{0,2,1:T(8,128)} %fusion.6) | data formatting | bytes 28311552 | tf_op jit(solution)/shard_map/stack | solution.py:120
  128.1 0.0 reduce-scatter.2.cloned.1.call-update
  128.1 18.3 %all-reduce.1 = (f32[256]{0:T(256)}, f32[256]{0:T(256)}, f32[3,256]{1,0:T(4,128)}, f32[]{:T(128)}) all-reduce(f32[256]{0:T(256)S(1)} %get-tuple-element.36, f32[256]{0:T(256)S(1)} %get-tuple-element.37, f32[3,256]{1,0:T(4,128)S(1)} %get-tuple-element.38, f32[]{:T(128)} %get-tuple-element.39), channel_id=1, replica_groups=mesh['rep'=8,'tile'=4] {'rep'}, use_global_device_ids=true, to_apply=%region_15.16 | all-reduce | flops 1281 | bytes 10248 | tf_op jit(solution)/shard_map/psum | solution.py:80
  147.1 7.8 %fusion.33 = f32[1728,1536]{1,0:T(8,128)} fusion(bf16[1728,256]{1,0:T(8,128)(2,1)S(1)} %multiply_convert_fusion, bf16[9,1536,256]{2,1,0:T(8,128)(2,1)} %param.10), kind=kOutput, calls=%fused_computation.52 | convolution fusion | flops 1358954496 | bytes 12288000 | tf_op jit(solution)/shard_map/dot_general | solution.py:105
  154.8 0.6 fusion.62
  155.5 8.2 %fusion.26 = f32[1728,1536]{1,0:T(8,128)} fusion(bf16[1728,256]{1,0:T(8,128)(2,1)S(1)} %bitcast.174, bf16[9,1536,256]{2,1,0:T(8,128)(2,1)} %param.10), kind=kOutput, calls=%fused_computation.45 | convolution fusion | flops 1358954496 | bytes 12288000 | tf_op jit(solution)/shard_map/dot_general | solution.py:105
  163.6 6.3 %fusion.29 = f32[1728,1536]{1,0:T(8,128)} fusion(bf16[1728,256]{1,0:T(8,128)(2,1)S(1)} %bitcast.173, bf16[9,1536,256]{2,1,0:T(8,128)(2,1)S(1)} %bitcast.167), kind=kOutput, calls=%fused_computation.48 | convolution fusion | flops 1358954496 | bytes 12288000 | tf_op jit(solution)/shard_map/dot_general | solution.py:105
  170.0 6.3 %fusion.31 = f32[1728,1536]{1,0:T(8,128)} fusion(bf16[1728,256]{1,0:T(8,128)(2,1)S(1)} %bitcast.172, bf16[9,1536,256]{2,1,0:T(8,128)(2,1)S(1)} %bitcast.167), kind=kOutput, calls=%fused_computation.50 | convolution fusion | flops 1358954496 | bytes 12288000 | tf_op jit(solution)/shard_map/dot_general | solution.py:105
  176.3 6.4 %fusion.35 = f32[1728,1536]{1,0:T(8,128)} fusion(bf16[1728,256]{1,0:T(8,128)(2,1)S(1)} %bitcast.171, bf16[9,1536,256]{2,1,0:T(8,128)(2,1)S(1)} %bitcast.167), kind=kOutput, calls=%fused_computation.54 | convolution fusion | flops 1358954496 | bytes 12288000 | tf_op jit(solution)/shard_map/dot_general | solution.py:105
  182.7 5.7 %fusion.37 = f32[1728,1536]{1,0:T(8,128)} fusion(bf16[1728,256]{1,0:T(8,128)(2,1)S(1)} %bitcast.170, bf16[9,1536,256]{2,1,0:T(8,128)(2,1)S(1)} %bitcast.167), kind=kOutput, calls=%fused_computation.56 | convolution fusion | flops 1358954496 | bytes 12288000 | tf_op jit(solution)/shard_map/dot_general | solution.py:105
  188.5 5.6 %fusion.41 = f32[1728,1536]{1,0:T(8,128)} fusion(bf16[1728,256]{1,0:T(8,128)(2,1)S(1)} %bitcast.169, bf16[9,1536,256]{2,1,0:T(8,128)(2,1)S(1)} %bitcast.167), kind=kOutput, calls=%fused_computation.60 | convolution fusion | flops 1358954496 | bytes 12288000 | tf_op jit(solution)/shard_map/dot_general | solution.py:105
  194.1 6.2 %fusion.39 = f32[1728,1536]{1,0:T(8,128)} fusion(bf16[1728,256]{1,0:T(8,128)(2,1)S(1)} %bitcast.164, bf16[9,1536,256]{2,1,0:T(8,128)(2,1)S(1)} %bitcast.167), kind=kOutput, calls=%fused_computation.58 | convolution fusion | flops 1358954496 | bytes 12288000 | tf_op jit(solution)/shard_map/dot_general | solution.py:105
  200.3 30.0 %add_convert_fusion = bf16[1728,1536]{1,0:T(8,128)(2,1)} fusion(f32[1728,1536]{1,0:T(8,128)} %fusion.26, f32[1728,1536]{1,0:T(8,128)} %fusion.29, f32[1728,1536]{1,0:T(8,128)} %fusion.31, f32[1728,1536]{1,0:T(8,128)} %fusion.33, f32[1728,1536]{1,0:T(8,128)} %fusion.35, f32[1728,1536]{1,0:T(8,128)} %fusion.37, f32[1728,1536]{1,0:T(8,128)} %fusion.41, ...), kind=kOutput, calls=%fused_computation.2 | convolution fusion | flops 1382842368 | bytes 91914240 | tf_op jit(solution)/shard_map/dot_general | solution.py:105
  230.3 149.6 %reduce-scatter.2.cloned.1.call-done = f32[48,9,256]{2,1,0:T(8,128)} async-done(((f32[1536,9,256]{2,1,0:T(8,128)}), f32[48,9,256]{2,1,0:T(8,128)}) %reduce-scatter.2.cloned.1.call-update) | async-done | bytes 442384 | tf_op jit(solution)/shard_map/reduce_scatter | solution.py:119
  379.9 2.2 copy.19
  (28 shorter events, 0.1 us)
Async XLA Ops:
  7.2 20.6 %copy-start = (f32[3,256]{1,0:T(4,128)S(1)}, f32[3,256]{1,0:T(4,128)}, u32[]{:S(2)}) copy-start(f32[3,256]{1,0:T(4,128)} %param.13) | copy-start | bytes 9220
  7.2 53.7 %copy-start.6 = (f32[256]{0:T(256)S(1)}, f32[256]{0:T(256)}, u32[]{:S(2)}) copy-start(f32[256]{0:T(256)} %param.11) | copy-start | bytes 3076
  7.2 53.7 %copy-start.7 = (f32[256]{0:T(256)S(1)}, f32[256]{0:T(256)}, u32[]{:S(2)}) copy-start(f32[256]{0:T(256)} %param.12) | copy-start | bytes 3076
  7.2 372.7 %reduce-scatter.2.cloned.1.call-start = ((), (), s32[]{:S(2)}) async-start(), calls=%async_computation.1 | async-start | bytes 25952256 | tf_op jit(solution)/shard_map/reduce_scatter | solution.py:119
  61.9 22.2 %slice-start = ((s8[5308416]{0:T(1024)(128)(4,1)}), s8[1114112]{0:T(1024)(128)(4,1)S(1)}, s32[]{:S(2)}) async-start(s8[5308416]{0:T(1024)(128)(4,1)} %bitcast.158), calls=%async_computation.2 | async-start | bytes 2228224
  72.8 11.3 %slice-start.1 = ((s8[5308416]{0:T(1024)(128)(4,1)}), s8[4194304]{0:T(1024)(128)(4,1)S(1)}, s32[]{:S(2)}) async-start(s8[5308416]{0:T(1024)(128)(4,1)} %bitcast.158), calls=%async_computation.3 | async-start | bytes 8388608
  75.2 3.8 collective-permute-start
  77.0 5.3 %collective-permute-start.1 = (bf16[2,12,72,256]{3,2,1,0:T(8,128)(2,1)S(1)}, bf16[2,12,72,256]{3,2,1,0:T(8,128)(2,1)S(1)}, u32[]{:S(2)}, u32[]{:S(2)}) collective-permute-start(bf16[2,12,72,256]{3,2,1,0:T(8,128)(2,1)S(1)} %bitcast.161), channel_id=1, source_target_pairs={{1,0},{2,1},{3,2},{5,4},{6,5},{7,6},{9,8},{10,9},{11,10},{13,12},{... | collective-permute-start | bytes 2654216 | tf_op jit(solution)/shard_map/ppermute | solution.py:25
  78.9 24.6 %copy-start.4 = (bf16[2,12,72,256]{3,2,1,0:T(8,128)(2,1)}, bf16[2,12,72,256]{3,2,1,0:T(8,128)(2,1)S(1)}, u32[]{:S(2)}) copy-start(bf16[2,12,72,256]{3,2,1,0:T(8,128)(2,1)S(1)} %collective-permute-done) | copy-start | bytes 2654212
  84.1 22.2 %copy-start.2 = (bf16[2,36,96,256]{3,2,1,0:T(8,128)(2,1)}, bf16[2,36,96,256]{3,2,1,0:T(8,128)(2,1)S(1)}, u32[]{:S(2)}) copy-start(bf16[2,36,96,256]{3,2,1,0:T(8,128)(2,1)S(1)} %fusion.5) | copy-start | bytes 10616836
  147.1 7.8 %copy-start.3 = (bf16[2,36,96,256]{3,2,1,0:T(8,128)(2,1)S(1)}, bf16[2,36,96,256]{3,2,1,0:T(8,128)(2,1)}, u32[]{:S(2)}) copy-start(bf16[2,36,96,256]{3,2,1,0:T(8,128)(2,1)} %copy-done.2) | copy-start | bytes 10616836
  154.8 8.8 %slice-start.2 = ((s8[7077888]{0:T(1024)(128)(4,1)}), s8[2883584]{0:T(1024)(128)(4,1)S(1)}, s32[]{:S(2)}) async-start(s8[7077888]{0:T(1024)(128)(4,1)} %bitcast.166), calls=%async_computation.4 | async-start | bytes 5767168
  155.4 8.2 %slice-start.3 = ((s8[7077888]{0:T(1024)(128)(4,1)}), s8[4194304]{0:T(1024)(128)(4,1)S(1)}, s32[]{:S(2)}) async-start(s8[7077888]{0:T(1024)(128)(4,1)} %bitcast.166), calls=%async_computation.5 | async-start | bytes 8388608
  194.1 6.2 %copy-start.5 = (bf16[2,12,72,256]{3,2,1,0:T(8,128)(2,1)S(1)}, bf16[2,12,72,256]{3,2,1,0:T(8,128)(2,1)}, u32[]{:S(2)}) copy-start(bf16[2,12,72,256]{3,2,1,0:T(8,128)(2,1)} %copy-done.4) | copy-start | bytes 2654212
  200.3 181.8 %copy-start.1 = (f32[3,256]{1,0:T(4,128)S(1)}, f32[3,256]{1,0:T(4,128)}, u32[]{:S(2)}) copy-start(f32[3,256]{1,0:T(4,128)} %param.13) | copy-start | bytes 9220
Sparse Core Ops, SparseCore 0:
  128.2 251.6 reduce-scatter.1
